TPU v7x, 128 devices: a whole 4x4x4 slice. The times are simulated.
128 devices in a mesh: band: 4 (over x), pair: 32 (over z, y, core).
Axes of the slice: x: 4, y: 4, z: 4, core: 2. Of those that a mesh axis runs over, the one named last changes fastest.
Arguments:
- traces: float32 [16, 8192, 1024], P('band', 'pair'), may hold values from -300 to 300
- pair_list: int32 [256, 2], replicated, may hold values from 0 to 63, as said below
- pair_owner: int32 [256], replicated, may hold values from 0 to 63, as said below
Outputs:
- cross_spectra: bfloat16 [64, 2, 128, 128, 512], P('pair', None, None, None, 'band')
Inputs may be any that keep to these rules, and one draw needn't show every extreme that they name: `pair_list`: each row (i, j) has 8 <= j - i <= 24; index p of pair holds blocks p * 64 / 32 up to (p + 1) * 64 / 32 - 1, and the 16 blocks named by the rows of one owner (pair_owner // 2) all lie on different indices of pair. `pair_owner`: every slot is named by exactly 4 rows.
All inputs are finite; a program needn't handle non-finite values.
Results may differ from a plain program's by a relative error of at most 0.0057.
Values may be sent and summed in bfloat16 or wider, within the bound.
No kernel may reach another device: no remote copies, remote signals or barrier semaphores. Data moves between devices by JAX's collectives and lax.ppermute only.
A program may use at most 320 MiB of HBM per device.

v0:
```python
import numpy as np
import jax
import jax.numpy as jnp
from jax import lax
from jax.sharding import PartitionSpec as P

SUB = 64
BLOCK = 128
SLOTS = 2
whiten_eps = 1e-05


def dft_table(samples, bins):
    phase_angle = np.arange(samples)[None, :] * bins[:, None] % samples * (2.0 * np.pi / samples)
    return jnp.asarray(
        np.concatenate([np.cos(phase_angle), -np.sin(phase_angle)], axis=0).astype(np.float32)
    )


def whiten(flat_traces, bins):
    row_count, samples = flat_traces.shape
    bin_count = bins.shape[0]
    spectra = lax.dot_general(
        dft_table(samples, bins),
        flat_traces,
        (((1,), (1,)), ((), ())),
        precision=lax.Precision.HIGH,
        preferred_element_type=jnp.float32,
    )
    real_band = spectra[:bin_count].reshape(bin_count // SUB, SUB, row_count)
    imag_band = spectra[bin_count:].reshape(bin_count // SUB, SUB, row_count)
    band_power = jnp.mean(real_band * real_band + imag_band * imag_band, axis=1, keepdims=True)
    factor = lax.rsqrt(band_power + whiten_eps)
    stacked = jnp.stack([real_band * factor, imag_band * factor], axis=0)
    return stacked.reshape(2, bin_count, row_count).astype(jnp.bfloat16)


def slot_blocks(pair_list, pair_owner, slot_ids, per_slot):
    slot_match = (pair_owner[:, None] == slot_ids[None, :]).astype(jnp.int32)
    slot_rank = jnp.cumsum(slot_match, axis=0) - 1
    rank_ids = jnp.arange(per_slot, dtype=jnp.int32)
    selected = slot_match[:, :, None] * (slot_rank[:, :, None] == rank_ids[None, None, :]).astype(
        jnp.int32
    )
    first = jnp.sum(selected * pair_list[:, 0][:, None, None], axis=0)
    second = jnp.sum(selected * pair_list[:, 1][:, None, None], axis=0)
    return (first, second)


def shards(traces, pair_list, pair_owner):
    win_local, chan_local, samples = traces.shape
    bin_count = samples // 2
    bands = lax.axis_size("band")
    owners = lax.axis_size("pair")
    band_bins = bin_count // bands
    per_device = chan_local // BLOCK
    per_slot = pair_list.shape[0] // (owners * SLOTS)
    flat = traces.reshape(win_local * chan_local, samples)
    halves = 2
    half_bins = band_bins // halves
    edges = [0, band_bins // 2, 3 * band_bins // 4, band_bins]
    spans = []
    for half in range(halves):
        ids = np.arange(bands * half_bins)
        bins = ids // half_bins * band_bins + half * half_bins + ids % half_bins
        whitened = whiten(flat, bins)
        whitened = whitened.reshape(2, bands, half_bins, win_local, per_device, BLOCK)
        spans.append(jnp.transpose(whitened, (1, 4, 0, 3, 2, 5)))
    pieces = []
    for low, high in zip(edges[:-1], edges[1:]):
        parts = []
        for half in range(halves):
            start = max(low, half * half_bins)
            stop = min(high, (half + 1) * half_bins)
            if start < stop:
                parts.append(
                    spans[half][:, :, :, :, start - half * half_bins : stop - half * half_bins, :]
                )
        chunk_bins = parts[0] if len(parts) == 1 else jnp.concatenate(parts, axis=4)
        pieces.append(lax.all_to_all(chunk_bins, "band", split_axis=0, concat_axis=0, tiled=True))
    chunks = len(pieces)
    device_index = lax.axis_index("pair")
    slot_ids = device_index * SLOTS + jnp.arange(SLOTS, dtype=jnp.int32)
    first, second = slot_blocks(pair_list, pair_owner, slot_ids, per_slot)
    wanted = jnp.concatenate([first.reshape(-1), second.reshape(-1)])
    picks = (wanted[:, None] == jnp.arange(owners * per_device, dtype=jnp.int32)[None, :]).astype(
        jnp.bfloat16
    )
    products = []
    for part in range(chunks):
        piece = jnp.transpose(pieces[part], (1, 0, 2, 3, 4, 5))
        gathered = lax.all_gather(piece, "pair", axis=0, tiled=True)
        if part == chunks - 1 and part >= 1:
            gathered, products[-1] = lax.optimization_barrier((gathered, products[-1]))
        rows = gathered.shape[0]
        chosen = jnp.dot(picks, gathered.reshape(rows, -1), preferred_element_type=jnp.bfloat16)
        chosen = chosen.reshape(2, SLOTS, per_slot, *gathered.shape[1:])
        left = chosen[0]
        right = chosen[1]
        rotated = jnp.stack([-right[:, :, :, 1], right[:, :, :, 0]], axis=3)
        paired = jnp.stack([right, rotated], axis=1)
        product = jnp.einsum(
            "stgkwfa,sptgkwfb->spabf", left, paired, preferred_element_type=jnp.float32
        )
        product = product.astype(jnp.bfloat16)
        if part + 2 < chunks:
            pieces[part + 2], product = lax.optimization_barrier((pieces[part + 2], product))
        products.append(product)
    out = jnp.zeros((SLOTS, 2, BLOCK, BLOCK, band_bins), jnp.bfloat16)
    for part in range(chunks):
        out = lax.dynamic_update_slice_in_dim(out, products[part], edges[part], axis=4)
    return out


def solution(mesh):
    placed = (P("band", "pair", None), P(), P())
    return jax.shard_map(
        shards,
        mesh=mesh,
        in_specs=placed,
        out_specs=P("pair", None, None, None, "band"),
        check_vma=False,
    )
```

profile of v0, /device:TPU:1, one launch (start us, length us, event | category | flops | bytes accessed | tf_op | source)
XLA Modules:
  0.0 361.0 jit_solution(15198788224465309761)
XLA Ops:
  6.5 6.3 %fusion.52 = f32[512,1024]{1,0:T(8,128)S(1)} fusion(f32[512,1024]{1,0:T(8,128)} %constant.33.clone, f32[1024,1024]{1,0:T(8,128)} %bitcast.142), kind=kOutput, calls=%fused_computation.85 | convolution fusion | flops 3221225472 | bytes 8388608 | tf_op jit(solution)/shard_map/dot_general | solution.py:23
  14.5 19.0 %all_to_all.15 = bf16[4,2,2,4,64,128]{5,4,3,2,1,0:T(8,128)(2,1)S(1)} all-to-all(bf16[4,2,2,4,64,128]{5,4,3,2,1,0:T(8,128)(2,1)S(1)} %maximum_bitcast_fusion.4), channel_id=1, replica_groups=mesh['band'=4,'pair'=32] {'band'}, dimensions={0} | all-to-all | bytes 2097152 | tf_op jit(solution)/shard_map/all_to_all | solution.py:80
  34.7 5.7 %fusion.51 = f32[512,1024]{1,0:T(8,128)S(1)} fusion(f32[512,1024]{1,0:T(8,128)S(1)} %copy-done.1, f32[1024,1024]{1,0:T(8,128)} %bitcast.143), kind=kOutput, calls=%fused_computation.84 | convolution fusion | flops 3221225472 | bytes 8388608 | tf_op jit(solution)/shard_map/dot_general | solution.py:23
  42.9 10.1 %all_to_all.16 = bf16[4,2,2,4,32,128]{5,4,3,2,1,0:T(8,128)(2,1)S(1)} all-to-all(bf16[4,2,2,4,32,128]{5,4,3,2,1,0:T(8,128)(2,1)S(1)} %get-tuple-element.31), channel_id=1, replica_groups=mesh['band'=4,'pair'=32] {'band'}, dimensions={0} | all-to-all | bytes 1048576 | tf_op jit(solution)/shard_map/all_to_all | solution.py:80
  54.0 3.5 all-to-all-start
  59.5 91.2 %all-gather.4.cloned.1.call-done = bf16[64,4,2,4,64,128]{5,4,3,2,1,0:T(8,128)(2,1)} async-done(((bf16[2,4,2,4,64,128]{5,4,3,2,1,0:T(8,128)(2,1)}), bf16[64,4,2,4,64,128]{5,4,3,2,1,0:T(8,128)(2,1)}) %all-gather.4.cloned.1.call-update) | async-done | bytes 33554448 | tf_op jit(solution)/shard_map/all_gather | solution.py:92
  150.7 26.2 %fusion = bf16[16,262144]{1,0:T(8,128)(2,1)S(1)} fusion(bf16[8,8,2048,128]{3,2,1,0:T(8,128)(2,1)} %bitcast.133, s32[16]{0:T(128)S(1)} %pad_add_fusion), kind=kOutput, calls=%fused_computation | convolution fusion | flops 536871936 | bytes 41943104 | tf_op jit(solution)/shard_map/dot_general | solution.py:96
  176.8 1.2 slice_bitcast_fusion
  179.1 3.2 copy.66
  183.4 1.6 copy.92
  185.1 2.1 copy_negate_fusion
  187.2 2.9 maximum_bitcast_fusion
  190.1 17.0 %fusion.9 = bf16[2,2,128,128,64]{2,3,1,4,0:T(8,128)(2,1)} fusion(bf16[2,1,4,4,2,4,64,128]{7,5,2,4,3,1,6,0:T(4,128)(2,1)S(1)} %maximum_bitcast_fusion, bf16[2,1,4,4,2,4,64,128]{7,5,2,4,3,1,6,0:T(4,128)(2,1)S(1)} %copy.66, bf16[2,4,4,2,4,64,128,1]{6,5,4,3,2,1,0,7:T(8,128)(2,1)S(1)} %bitcast.144), kind=kOutput, calls=%fused_computation.10 | convolution fusion | flops 1094713344 | bytes 20971520 | tf_op jit(solution)/shard_map/stgkwfa,sptgkwfb->spabf/dot_general | solution.py:102
  208.0 16.9 %all-gather.8.cloned.1.call-done = bf16[64,4,2,4,32,128]{5,4,3,2,1,0:T(8,128)(2,1)} async-done(((bf16[2,4,2,4,32,128]{5,4,3,2,1,0:T(8,128)(2,1)}), bf16[64,4,2,4,32,128]{5,4,3,2,1,0:T(8,128)(2,1)}) %all-gather.8.cloned.1.call-update) | async-done | bytes 16777232 | tf_op jit(solution)/shard_map/all_gather | solution.py:92
  224.9 14.9 %fusion.6 = bf16[16,131072]{1,0:T(8,128)(2,1)S(1)} fusion(bf16[8,8,1024,128]{3,2,1,0:T(8,128)(2,1)} %bitcast.140, s32[16]{0:T(128)S(1)} %pad_add_fusion), kind=kOutput, calls=%fused_computation.6 | convolution fusion | flops 268436480 | bytes 20971584 | tf_op jit(solution)/shard_map/dot_general | solution.py:96
  243.8 1.4 maximum_bitcast_fusion.1
  245.1 6.3 %fusion.16 = bf16[2,2,128,128,32]{2,3,1,4,0:T(8,128)(2,1)} fusion(bf16[2,1,4,4,2,4,32,128]{7,5,2,4,3,1,6,0:T(4,128)(2,1)S(1)} %maximum_bitcast_fusion.1, bf16[2,1,4,4,2,4,32,128]{7,5,2,4,3,1,6,0:T(4,128)(2,1)S(1)} %copy.72, bf16[2,4,4,2,4,32,128,1]{6,5,4,3,2,1,0,7:T(8,128)(2,1)S(1)} %bitcast.147), kind=kOutput, calls=%fused_computation.17 | convolution fusion | flops 547356672 | bytes 10485760 | tf_op jit(solution)/shard_map/stgkwfa,sptgkwfb->spabf/dot_general | solution.py:102
  251.4 10.0 %dynamic_update_slice.9 = bf16[2,2,128,128,128]{2,3,1,4,0:T(8,128)(2,1)} pad(bf16[2,2,128,128,64]{2,3,1,4,0:T(8,128)(2,1)} %fusion.9, bf16[]{:T(256)} %constant.30.clone.1), padding=0_0x0_0x0_0x0_0x0_64 | pad | bytes 25165826 | tf_op jit(solution)/shard_map/dynamic_update_slice | solution.py:111
  261.4 37.8 %all-gather.6.cloned.1.call-done = bf16[64,4,2,4,32,128]{5,4,3,2,1,0:T(8,128)(2,1)} async-done(((bf16[2,4,2,4,32,128]{5,4,3,2,1,0:T(8,128)(2,1)}), bf16[64,4,2,4,32,128]{5,4,3,2,1,0:T(8,128)(2,1)}) %all-gather.6.cloned.1.call-update) | async-done | bytes 16777232 | tf_op jit(solution)/shard_map/all_gather | solution.py:92
  299.3 14.9 %fusion.3 = bf16[16,131072]{1,0:T(8,128)(2,1)S(1)} fusion(bf16[8,8,1024,128]{3,2,1,0:T(8,128)(2,1)} %bitcast.141, s32[16]{0:T(128)S(1)} %pad_add_fusion), kind=kOutput, calls=%fused_computation.3 | convolution fusion | flops 268436480 | bytes 20971584 | tf_op jit(solution)/shard_map/dot_general | solution.py:96
  318.1 1.4 maximum_bitcast_fusion.2
  319.5 2.8 constant_dynamic-update-slice_fusion
  322.3 6.2 %fusion.18 = bf16[2,2,128,128,128]{2,3,1,4,0:T(8,128)(2,1)} fusion(bf16[2,2,128,128,128]{2,3,1,4,0:T(8,128)(2,1)} %constant_dynamic-update-slice_fusion, bf16[2,1,4,4,2,4,32,128]{7,5,2,4,3,1,6,0:T(4,128)(2,1)S(1)} %maximum_bitcast_fusion.2, bf16[2,1,4,4,2,4,32,128]{7,5,2,4,3,1,6,0:T(4,128)(2,1)S(1)} %copy.76, ...), kind=kOutput, calls=%fused_computation.19 | convolution fusion | flops 547356672 | bytes 10485760 | tf_op jit(solution)/shard_map/stgkwfa,sptgkwfb->spabf/dot_general | solution.py:102
  328.5 25.8 %copy.78 = bf16[2,2,128,128,128]{4,3,2,1,0:T(8,128)(2,1)} copy(bf16[2,2,128,128,128]{2,3,1,4,0:T(8,128)(2,1)} %fusion.18) | data formatting | bytes 33554432 | tf_op jit(solution)/shard_map/dynamic_update_slice | solution.py:111
  (65 shorter events, 18.9 us)
Async XLA Ops:
  6.5 144.1 %all-gather.4.cloned.1.call-start = ((), (), s32[]{:S(2)}) async-start(), calls=%async_computation.3 | async-start | bytes 34603008 | tf_op jit(solution)/shard_map/all_gather | solution.py:92
  14.5 20.1 %copy-start.1 = (f32[512,1024]{1,0:T(8,128)S(1)}, f32[512,1024]{1,0:T(8,128)}, u32[]{:S(2)}) copy-start(f32[512,1024]{1,0:T(8,128)} %constant.34.clone) | copy-start | bytes 6291460
  34.6 190.3 %all-gather.8.cloned.1.call-start = ((), (), s32[]{:S(2)}) async-start(), calls=%async_computation.5 | async-start | bytes 17301504 | tf_op jit(solution)/shard_map/all_gather | solution.py:92
  41.9 15.9 %copy-start.2 = (s32[256]{0:T(256)S(1)}, s32[256]{0:T(256)}, u32[]{:S(2)}) copy-start(s32[256]{0:T(256)} %param.7) | copy-start | bytes 3076
  41.9 17.2 %copy-start.3 = (s32[256,2]{0,1:T(2,128)S(1)}, s32[256,2]{0,1:T(2,128)}, u32[]{:S(2)}) copy-start(s32[256,2]{0,1:T(2,128)} %param.6) | copy-start | bytes 6148
  54.0 153.2 %all-to-all-start = ((bf16[4,2,2,4,32,128]{5,4,3,2,1,0:T(8,128)(2,1)}), bf16[4,2,2,4,32,128]{5,4,3,2,1,0:T(8,128)(2,1)S(1)}, u32[]{:S(2)}, u32[]{:S(2)}) async-start(bf16[4,2,2,4,32,128]{5,4,3,2,1,0:T(8,128)(2,1)} %get-tuple-element.32), calls=%async_computation | async-start | bytes 1048576 | tf_op jit(solution)/shard_map/all_to_all | solution.py:80
  57.4 241.8 %all-gather.6.cloned.1.call-start = ((), (), s32[]{:S(2)}) async-start(), calls=%async_computation.4 | async-start | bytes 17301504 | tf_op jit(solution)/shard_map/all_gather | solution.py:92
  316.8 2.7 copy-start
Sparse Core Ops, SparseCore 0:
  34.7 115.8 all-gather.3
  152.9 71.9 all-gather.7
  227.1 72.0 all-gather.5
where the time goes:
time: 368 us; the launch traced here: 361 us
  waiting for transfers between devices  146 us (40%)
  matrix products  97.5 us (26%)
  local copies, waits for them, and re-layouts  59.3 us (16%)
  blocking collectives  29.1 us (8%)
  between operations  13.7 us (4%)
  other arithmetic  11.6 us (3%)
  starting transfers between devices  3.87 us (1%)
    all_gather x3, waiting for transfers between devices, shards(): gathered = lax.all_gather(piece, 'pair', axis=0, tiled=True)  146 us
    dot_general x3, matrix products, shards(): jnp.dot(picks, gathered.reshape(rows, -1), preferred_element_type=jnp.bfl...  56 us
    dynamic_update_slice x3, local copies, waits for them, and re-layouts, shards(): lax.dynamic_update_slice_in_dim(out, products[part], edges[part], axis=4)  38.7 us
    dot_general x3, matrix products, shards(): jnp.einsum('stgkwfa,sptgkwfb->spabf', left, paired, preferred_element_typ...  29.5 us
    all_to_all x2, blocking collectives, shards(): lax.all_to_all(chunk_bins, 'band', split_axis=0, concat_axis=0, tiled=True)  29.1 us
    dot_general x2, matrix products, whiten(): lax.dot_general(dft_table(samples, bins), flat_traces, (((1,), (1,)), (()...  12 us
  transfers between devices with their start and end apart: 4, of which 3 were waited for; matrix products, arithmetic and copies ran while one was open for 29% of the time, Pallas kernels for 0%

commit v1 on v0

--- a/solution.py
+++ b/solution.py
@@ -8,6 +8,13 @@
 BLOCK = 128
 SLOTS = 2
 whiten_eps = 1e-05
+
+
+def _close_ranges(block_here, mesh_ax):
+    near = jnp.concatenate(
+        lax.all_to_all(jnp.stack(lax.psum(1, mesh_ax) * [block_here]), mesh_ax, 0, 0), axis=0
+    )
+    return near
 
 
 def dft_table(samples, bins):
@@ -89,7 +96,7 @@
     products = []
     for part in range(chunks):
         piece = jnp.transpose(pieces[part], (1, 0, 2, 3, 4, 5))
-        gathered = lax.all_gather(piece, "pair", axis=0, tiled=True)
+        gathered = _close_ranges(piece, "pair")
         if part == chunks - 1 and part >= 1:
             gathered, products[-1] = lax.optimization_barrier((gathered, products[-1]))
         rows = gathered.shape[0]

time: 368 us -> 1030 us (2.80); the launches traced: 361 us -> 1010 us
  waiting for transfers between devices: 146 us -> 685 us
  local copies, waits for them, and re-layouts: 59.3 us -> 131 us
  starting transfers between devices: 3.87 us -> 65.1 us
  other arithmetic: 11.6 us -> 27.2 us
  matrix products: 97.5 us -> 82.1 us
  between operations: 13.7 us -> 0.84 us
  blocking collectives: 29.1 us -> 17.5 us
    all_to_all x0 -> x3, waiting for transfers between devices: none -> 679 us  [_close_ranges(): lax.all_to_all(jnp.stack(lax.psum(1, mesh_ax) * [block_here]), mesh_ax, 0...]
    all_gather x3 -> x0, waiting for transfers between devices: 146 us -> none  [shards(): gathered = lax.all_gather(piece, 'pair', axis=0, tiled=True)]
    another operation x0 -> x5, local copies, waits for them, and re-layouts: none -> 68.7 us  [the longest x2 44.9 us: shards(): gathered.reshape(rows, -1)]
    all_to_all x0 -> x3, starting transfers between devices: none -> 56.8 us  [_close_ranges(): lax.all_to_all(jnp.stack(lax.psum(1, mesh_ax) * [block_here]), mesh_ax, 0...]
    dot_general x3, matrix products: 56 us -> 39.4 us  [shards(): jnp.dot(picks, gathered.reshape(rows, -1), preferred_element_type=jnp.bfl...]
    another operation x3, other arithmetic: 5.58 us -> 18.6 us  [shards(): paired = jnp.stack([right, rotated], axis=1)]
    all_to_all x2 -> x1, blocking collectives: 29.1 us -> 17.5 us  [shards(): lax.all_to_all(chunk_bins, 'band', split_axis=0, concat_axis=0, tiled=True)]
  transfers between devices with their start and end apart: 4 -> 5, of which waited for: 3 -> 4; matrix products, arithmetic and copies ran while one was open for 29% -> 15% of each run, Pallas kernels for 0% -> 0%
where the time goes in v1:
time: 1030 us; the launch traced here: 1010 us
  waiting for transfers between devices  685 us (67%)
  local copies, waits for them, and re-layouts  131 us (13%)
  matrix products  82.1 us (8%)
  starting transfers between devices  65.1 us (6%)
  other arithmetic  27.2 us (3%)
  blocking collectives  17.5 us (2%)
    all_to_all x3, waiting for transfers between devices, _close_ranges(): lax.all_to_all(jnp.stack(lax.psum(1, mesh_ax) * [block_here]), mesh_ax, 0...  679 us
    all_to_all x3, starting transfers between devices, _close_ranges(): lax.all_to_all(jnp.stack(lax.psum(1, mesh_ax) * [block_here]), mesh_ax, 0...  56.8 us
    another operation x2, local copies, waits for them, and re-layouts, shards(): gathered.reshape(rows, -1)  44.9 us
    dot_general x3, matrix products, shards(): jnp.dot(picks, gathered.reshape(rows, -1), preferred_element_type=jnp.bfl...  39.4 us
    dynamic_update_slice x3, local copies, waits for them, and re-layouts, shards(): lax.dynamic_update_slice_in_dim(out, products[part], edges[part], axis=4)  38.9 us
    dot_general x3, matrix products, shards(): jnp.einsum('stgkwfa,sptgkwfb->spabf', left, paired, preferred_element_typ...  30.7 us
    another operation x3, local copies, waits for them, and re-layouts, _close_ranges(): jnp.stack(lax.psum(1, mesh_ax) * [block_here])  23.8 us
  transfers between devices with their start and end apart: 5, of which 4 were waited for; matrix products, arithmetic and copies ran while one was open for 15% of the time, Pallas kernels for 0%

profile of v1, /device:TPU:1, one launch (start us, length us, event | category | flops | bytes accessed | tf_op | source)
XLA Modules:
  0.0 1008.8 jit_solution(11864985722350135504)
XLA Ops:
  0.0 6.3 fusion.47
  15.8 5.7 fusion.48
  24.3 17.5 %all_to_all.30 = bf16[4,2,2,4,64,128]{5,1,3,4,2,0:T(2,128)(2,1)S(1)} all-to-all(bf16[4,2,2,4,64,128]{5,1,3,4,2,0:T(2,128)(2,1)S(1)} %maximum_bitcast_fusion.4), channel_id=1, replica_groups=mesh['band'=4,'pair'=32] {'band'}, dimensions={0} | all-to-all | bytes 2097152 | tf_op jit(solution)/shard_map/all_to_all | solution.py:87
  45.5 6.6 all-to-all-done.4
  52.1 11.2 %stack.42 = bf16[32,2,4,2,4,64,128]{6,5,4,3,2,1,0:T(8,128)(2,1)} broadcast(bf16[2,4,2,4,64,128]{5,4,3,2,1,0:T(8,128)(2,1)S(1)} %copy.65), dimensions={1,2,3,4,5,6} | broadcast | bytes 34603008 | tf_op jit(solution)/shard_map/stack | solution.py:15
  63.4 12.5 %all-to-all-start.2 = ((bf16[32,2,4,2,4,64,128]{6,5,4,3,2,1,0:T(8,128)(2,1)}), bf16[32,2,4,2,4,64,128]{6,5,4,3,2,1,0:T(8,128)(2,1)}, u32[]{:S(2)}, u32[]{:S(2)}) async-start(bf16[32,2,4,2,4,64,128]{6,5,4,3,2,1,0:T(8,128)(2,1)} %stack.42), calls=%async_computation.2 | async-start | bytes 67108864 | tf_op jit(solution)/shard_map/all_to_all | solution.py:15
  76.0 416.6 %all-to-all-done.2 = bf16[32,2,4,2,4,64,128]{6,5,4,3,2,1,0:T(8,128)(2,1)} async-done(((bf16[32,2,4,2,4,64,128]{6,5,4,3,2,1,0:T(8,128)(2,1)}), bf16[32,2,4,2,4,64,128]{6,5,4,3,2,1,0:T(8,128)(2,1)}, u32[]{:S(2)}, u32[]{:S(2)}) %all-to-all-start.2) | async-done | bytes 33554464 | tf_op jit(solution)/shard_map/all_to_all | solution.py:15
  492.6 6.4 stack.47
  498.9 27.5 %all-to-all-start.5 = ((bf16[32,2,4,2,4,32,128]{6,5,4,3,2,1,0:T(8,128)(2,1)}), bf16[32,2,4,2,4,32,128]{6,5,4,3,2,1,0:T(8,128)(2,1)}, u32[]{:S(2)}, u32[]{:S(2)}) async-start(bf16[32,2,4,2,4,32,128]{6,5,4,3,2,1,0:T(8,128)(2,1)} %stack.47), calls=%async_computation.5 | async-start | bytes 33554432 | tf_op jit(solution)/shard_map/all_to_all | solution.py:15
  528.1 28.2 %reshape_reshape.6 = bf16[64,262144]{1,0:T(8,128)(2,1)} reshape(bf16[32,2,4,2,4,64,128]{6,5,4,3,2,1,0:T(8,128)(2,1)} %all-to-all-done.2) | data formatting | bytes 67108864 | tf_op jit(solution)/shard_map/reshape;reshape | solution.py:103
  556.3 16.4 %fusion.35 = bf16[16,262144]{1,0:T(8,128)(2,1)} fusion(bf16[64,262144]{1,0:T(8,128)(2,1)} %reshape_reshape.6, s32[16]{0:T(128)S(1)} %pad_add_fusion), kind=kOutput, calls=%fused_computation.59 | convolution fusion | flops 536871936 | bytes 41943104 | tf_op jit(solution)/shard_map/dot_general | solution.py:103
  586.0 15.9 %maximum_bitcast_fusion = bf16[2,1,4,4,2,4,64,128]{7,5,2,4,3,1,6,0:T(4,128)(2,1)} fusion(bf16[2,4,4,1,4,64,128]{6,4,1,3,2,5,0:T(4,128)(2,1)S(1)} %copy.94, bf16[2,4,4,1,4,64,128]{6,4,1,3,2,5,0:T(4,128)(2,1)S(1)} %copy_negate_fusion), kind=kLoop, calls=%fused_computation.16 | loop fusion | flops 2097152 | bytes 8388608 | tf_op jit(solution)/shard_map/stack | solution.py:108
  601.9 18.3 %fusion.3 = bf16[2,2,128,128,64]{2,3,1,4,0:T(8,128)(2,1)} fusion(bf16[2,1,4,4,2,4,64,128]{7,5,2,4,3,1,6,0:T(4,128)(2,1)} %maximum_bitcast_fusion, bf16[2,1,4,4,2,4,64,128]{7,5,2,4,3,1,6,0:T(4,128)(2,1)S(1)} %copy.68, bf16[2,4,4,2,4,64,128,1]{6,5,4,3,2,1,0,7:T(8,128)(2,1)S(1)} %bitcast.142), kind=kOutput, calls=%fused_computation.4 | convolution fusion | flops 1094713344 | bytes 20971520 | tf_op jit(solution)/shard_map/stgkwfa,sptgkwfb->spabf/dot_general | solution.py:109
  621.3 106.7 %all-to-all-done.5 = bf16[32,2,4,2,4,32,128]{6,5,4,3,2,1,0:T(8,128)(2,1)} async-done(((bf16[32,2,4,2,4,32,128]{6,5,4,3,2,1,0:T(8,128)(2,1)}), bf16[32,2,4,2,4,32,128]{6,5,4,3,2,1,0:T(8,128)(2,1)}, u32[]{:S(2)}, u32[]{:S(2)}) %all-to-all-start.5) | async-done | bytes 16777248 | tf_op jit(solution)/shard_map/all_to_all | solution.py:15
  728.0 6.2 stack.46
  734.2 16.9 %all-to-all-start.3 = ((bf16[32,2,4,2,4,32,128]{6,5,4,3,2,1,0:T(8,128)(2,1)}), bf16[32,2,4,2,4,32,128]{6,5,4,3,2,1,0:T(8,128)(2,1)}, u32[]{:S(2)}, u32[]{:S(2)}) async-start(bf16[32,2,4,2,4,32,128]{6,5,4,3,2,1,0:T(8,128)(2,1)} %stack.46), calls=%async_computation.3 | async-start | bytes 33554432 | tf_op jit(solution)/shard_map/all_to_all | solution.py:15
  751.1 16.7 %reshape_reshape.7 = bf16[64,131072]{1,0:T(8,128)(2,1)} reshape(bf16[32,2,4,2,4,32,128]{6,5,4,3,2,1,0:T(8,128)(2,1)} %all-to-all-done.5) | data formatting | bytes 33554432 | tf_op jit(solution)/shard_map/reshape;reshape | solution.py:103
  767.7 8.1 fusion.34
  780.8 6.2 fusion.10
  787.1 10.2 %dynamic_update_slice.9 = bf16[2,2,128,128,128]{2,3,1,4,0:T(8,128)(2,1)} pad(bf16[2,2,128,128,64]{2,3,1,4,0:T(8,128)(2,1)} %fusion.3, bf16[]{:T(256)} %constant.30.clone.1), padding=0_0x0_0x0_0x0_0x0_64 | pad | bytes 25165826 | tf_op jit(solution)/shard_map/dynamic_update_slice | solution.py:118
  797.3 155.4 %all-to-all-done.3 = bf16[32,2,4,2,4,32,128]{6,5,4,3,2,1,0:T(8,128)(2,1)} async-done(((bf16[32,2,4,2,4,32,128]{6,5,4,3,2,1,0:T(8,128)(2,1)}), bf16[32,2,4,2,4,32,128]{6,5,4,3,2,1,0:T(8,128)(2,1)}, u32[]{:S(2)}, u32[]{:S(2)}) %all-to-all-start.3) | async-done | bytes 16777248 | tf_op jit(solution)/shard_map/all_to_all | solution.py:15
  952.7 14.9 %fusion = bf16[16,131072]{1,0:T(8,128)(2,1)S(1)} fusion(bf16[8,8,1024,128]{3,2,1,0:T(8,128)(2,1)} %bitcast.62, s32[16]{0:T(128)S(1)} %pad_add_fusion), kind=kOutput, calls=%fused_computation | convolution fusion | flops 268436480 | bytes 20971584 | tf_op jit(solution)/shard_map/dot_general | solution.py:103
  976.3 6.2 fusion.12
  982.5 25.8 %copy.80 = bf16[2,2,128,128,128]{4,3,2,1,0:T(8,128)(2,1)} copy(bf16[2,2,128,128,128]{2,3,1,4,0:T(8,128)(2,1)} %fusion.12) | data formatting | bytes 33554432 | tf_op jit(solution)/shard_map/dynamic_update_slice | solution.py:118
  (64 shorter events, 45.7 us)
Async XLA Ops:
  9.1 6.8 copy-start.1
  11.0 13.3 %all-to-all-start = ((bf16[4,2,2,4,32,128]{5,1,3,4,2,0:T(2,128)(2,1)}), bf16[4,2,2,4,32,128]{5,1,3,4,2,0:T(2,128)(2,1)}, u32[]{:S(2)}, u32[]{:S(2)}) async-start(bf16[4,2,2,4,32,128]{5,1,3,4,2,0:T(2,128)(2,1)} %get-tuple-element.32), calls=%async_computation | async-start | bytes 1048576 | tf_op jit(solution)/shard_map/all_to_all | solution.py:87
  41.8 10.4 %all-to-all-start.4 = ((bf16[4,2,2,4,32,128]{5,1,3,4,2,0:T(2,128)(2,1)}), bf16[4,2,2,4,32,128]{5,1,3,4,2,0:T(2,128)(2,1)S(1)}, u32[]{:S(2)}, u32[]{:S(2)}) async-start(bf16[4,2,2,4,32,128]{5,1,3,4,2,0:T(2,128)(2,1)} %get-tuple-element.31), calls=%async_computation.4 | async-start | bytes 1048576 | tf_op jit(solution)/shard_map/all_to_all | solution.py:87
  63.4 429.2 %all-to-all-start.2 = ((bf16[32,2,4,2,4,64,128]{6,5,4,3,2,1,0:T(8,128)(2,1)}), bf16[32,2,4,2,4,64,128]{6,5,4,3,2,1,0:T(8,128)(2,1)}, u32[]{:S(2)}, u32[]{:S(2)}) async-start(bf16[32,2,4,2,4,64,128]{6,5,4,3,2,1,0:T(8,128)(2,1)} %stack.42), calls=%async_computation.2 | async-start | bytes 67108864 | tf_op jit(solution)/shard_map/all_to_all | solution.py:15
  498.9 27.5 %copy-start.2 = (s32[256]{0:T(256)S(1)}, s32[256]{0:T(256)}, u32[]{:S(2)}) copy-start(s32[256]{0:T(256)} %param.7) | copy-start | bytes 3076
  498.9 28.7 %copy-start.3 = (s32[256,2]{0,1:T(2,128)S(1)}, s32[256,2]{0,1:T(2,128)}, u32[]{:S(2)}) copy-start(s32[256,2]{0,1:T(2,128)} %param.6) | copy-start | bytes 6148
  498.9 229.0 %all-to-all-start.5 = ((bf16[32,2,4,2,4,32,128]{6,5,4,3,2,1,0:T(8,128)(2,1)}), bf16[32,2,4,2,4,32,128]{6,5,4,3,2,1,0:T(8,128)(2,1)}, u32[]{:S(2)}, u32[]{:S(2)}) async-start(bf16[32,2,4,2,4,32,128]{6,5,4,3,2,1,0:T(8,128)(2,1)} %stack.47), calls=%async_computation.5 | async-start | bytes 33554432 | tf_op jit(solution)/shard_map/all_to_all | solution.py:15
  734.2 218.5 %all-to-all-start.3 = ((bf16[32,2,4,2,4,32,128]{6,5,4,3,2,1,0:T(8,128)(2,1)}), bf16[32,2,4,2,4,32,128]{6,5,4,3,2,1,0:T(8,128)(2,1)}, u32[]{:S(2)}, u32[]{:S(2)}) async-start(bf16[32,2,4,2,4,32,128]{6,5,4,3,2,1,0:T(8,128)(2,1)} %stack.46), calls=%async_computation.3 | async-start | bytes 33554432 | tf_op jit(solution)/shard_map/all_to_all | solution.py:15
  971.3 2.2 copy-start
